TPU v7x, 512 devices: a whole 4x8x8 slice. The times are simulated.
512 devices in a mesh: section: 8 (over z_lo, x), fsdp: 64 (over z_hi, y, core).
Axes of the slice: x: 4, y: 8, z: 8 (z_hi: 4, z_lo: 2; z = z_hi * 2 + z_lo), core: 2. Of those that a mesh axis runs over, the one named last changes fastest.
Arguments:
- activations: bfloat16 [10240, 6144], P('fsdp'), may hold values from -36 to 36
- keep: int32 [10240], P('fsdp'), may hold values from 0 to 1, as said below
- gains: bfloat16 [8, 6144], P('section'), may hold values from 0.099609375 to 1.8984375
- up_rows: int32 [8, 192, 2], P('section'), may hold values from 0 to 95
- up_blocks: bfloat16 [8, 384, 4096], P('section', 'fsdp'), may hold values from -0.5 to 0.5
- down_rows: int32 [8, 96, 2], P('section'), may hold values from 0 to 191
- down_blocks: bfloat16 [8, 192, 4096], P('section', 'fsdp'), may hold values from -0.5 to 0.5
Outputs:
- section_out: bfloat16 [8, 10240, 6144], P('section', 'fsdp')
Inputs may be any that keep to these rules, and one draw needn't show every extreme that they name: `keep`: each aligned block of 160 tokens (the tokens of one index of fsdp) holds exactly 128 ones.
All inputs are finite; a program needn't handle non-finite values.
Results may differ from a plain program's by a relative error of at most 0.012.
Values may be sent and summed in bfloat16 or wider, within the bound.
No kernel may reach another device: no remote copies, remote signals or barrier semaphores. Data moves between devices by JAX's collectives and lax.ppermute only.
A program may use at most 128 MiB of HBM per device.

v0:
```python
import jax
import jax.numpy as jnp
from jax import lax
from jax.sharding import Mesh
from jax.sharding import PartitionSpec as P

BLK = 64
UP_DEPTH = 2
DOWN_DEPTH = 2
KEEP_DEV = 128
SEC = ("zl", "x")
FS = ("zh", "y", "c")


def from_behind(value, axis, steps):
    count = lax.axis_size(axis)
    initial, last = (max(0, -steps), min(count, count - steps))
    return lax.ppermute(value, axis, [(source, source + steps) for source in range(initial, last)])


def exchange_zh(part):
    count = lax.axis_size("zh")
    own = lax.axis_index("zh")
    got = [part]
    for shift in range(1, count):
        got.append(lax.ppermute(part, "zh", [(i, (i + shift) % count) for i in range(count)]))
    stacked = jnp.stack(got)
    order = (own - jnp.arange(count, dtype=jnp.int32)) % count
    return jnp.take(stacked, order, axis=0)


def gather_up(shard):
    cols = shard.shape[1] // UP_DEPTH
    part = shard.reshape(cols, UP_DEPTH, BLK, BLK).transpose(0, 3, 1, 2)
    part = part.reshape(cols, BLK, UP_DEPTH * BLK)
    full = exchange_zh(part)
    full = lax.all_gather(full, ("y", "c"), axis=1, tiled=True)
    return full.reshape(-1, BLK, UP_DEPTH * BLK)


def gather_rows(shard):
    n = shard.shape[1]
    part = shard.reshape(n * 32, 128)
    full = exchange_zh(part)
    full = lax.all_gather(full, ("y", "c"), axis=1, tiled=True)
    return full.reshape(-1, 4096)


def make_layer(gain, up_index, up_values, down_index, down_values):
    width = gain.shape[0]
    hidden_width = up_values.shape[0] * BLK
    blocks_in = width // BLK
    blocks_hid = hidden_width // BLK
    weights_up = up_values
    weights_down = down_values.reshape(blocks_in, DOWN_DEPTH * BLK, BLK)
    gain_wide = gain.astype(jnp.float32)

    def layer(block):
        count = block.shape[0]
        wide = block.astype(jnp.float32)
        meansq = jnp.mean(wide * wide, axis=-1, keepdims=True)
        normed = (wide * lax.rsqrt(meansq + 1e-05) * gain_wide).astype(jnp.bfloat16)
        picked = normed.reshape(count, blocks_in, BLK)[:, up_index, :]
        picked = picked.reshape(count, blocks_hid, UP_DEPTH * BLK)
        up_sums = jnp.einsum("ncr,cjr->ncj", picked, weights_up, preferred_element_type=jnp.float32)
        hidden = jax.nn.gelu(up_sums, approximate=True).astype(jnp.bfloat16)
        second = hidden[:, down_index, :].reshape(count, blocks_in, DOWN_DEPTH * BLK)
        down_sums = jnp.einsum(
            "ncr,crj->ncj", second, weights_down, preferred_element_type=jnp.float32
        )
        return (wide + down_sums.reshape(count, width)).astype(jnp.bfloat16)

    return layer


def per_device(activations, keep, gains, up_rows, up_blocks, down_rows, down_blocks):
    up_all = gather_up(up_blocks)
    down_all = gather_rows(down_blocks)
    apply = make_layer(gains[0], up_rows[0].reshape(-1), up_all, down_rows[0].reshape(-1), down_all)
    places = jnp.cumsum(keep) - 1
    target = jnp.where(keep == 1, places, KEEP_DEV)
    chosen = (
        jnp.zeros((KEEP_DEV + 1,), jnp.int32)
        .at[target]
        .set(jnp.arange(keep.shape[0], dtype=jnp.int32))[:KEEP_DEV]
    )
    selected = activations[chosen]
    width = selected.shape[1]
    section = lax.axis_index(SEC)
    sections = lax.axis_size(SEC)
    pieces = 8
    group_rows = selected.shape[0] // pieces
    split = selected.reshape(pieces, group_rows, width)

    def advance(turn, held, record):
        offset = turn - section
        entry = jnp.where(section == 0, split[jnp.minimum(turn, pieces - 1)], held)
        active = (offset >= 0) & (offset < pieces)
        result = lax.cond(active, apply, jnp.zeros_like, entry)
        slot = jnp.clip(offset, 0, pieces - 1)
        current = lax.dynamic_index_in_dim(record, slot, 0, keepdims=False)
        updated = jnp.where(active, result, current)
        record = lax.dynamic_update_index_in_dim(record, updated, slot, 0)
        return (result, record)

    def turn_step(turn, carry):
        held, record = carry
        result, record = advance(turn, held, record)
        held = from_behind(result, SEC, 1)
        return (held, record)

    turns = sections + pieces - 1
    held, record = lax.fori_loop(0, turns, turn_step, (split[0], split))
    final = record.reshape(selected.shape[0], width)
    merged = activations.at[chosen].set(final)
    return merged[None]


def solution(mesh):
    zh = 4
    yc = mesh.shape["fsdp"] // zh
    zl = 2
    xs = mesh.shape["section"] // zl
    devices = mesh.devices.reshape(zl, xs, zh, yc // 2, 2)
    fine = Mesh(devices, ("zl", "x", "zh", "y", "c"))
    return jax.shard_map(
        per_device,
        mesh=fine,
        in_specs=(
            P(FS, None),
            P(FS),
            P(SEC, None),
            P(SEC, None, None),
            P(SEC, FS, None),
            P(SEC, None, None),
            P(SEC, FS, None),
        ),
        out_specs=P(SEC, FS, None),
        check_vma=False,
    )
```

profile of v0, /device:TPU:70, one launch (start us, length us, event | category | flops | bytes accessed | tf_op | source)
XLA Modules:
  0.0 516.3 jit_solution(16447429242946423552)
XLA Ops:
  8.2 6.1 %collective-permute-start.4 = (bf16[96,128]{1,0:T(8,128)(2,1)S(1)}, bf16[96,128]{1,0:T(8,128)(2,1)S(1)}, u32[]{:S(2)}, u32[]{:S(2)}) collective-permute-start(bf16[96,128]{1,0:T(8,128)(2,1)S(1)} %reshape.126), channel_id=1, source_target_pairs={{0,16},{16,32},{32,48},{48,0},{1,17},{17,33},{33,49},{49,1},{2,18}... | collective-permute-start | bytes 73736 | tf_op jit(solution)/shard_map/ppermute | solution.py:26
  14.3 8.2 %collective-permute-start.5 = (bf16[96,128]{1,0:T(8,128)(2,1)S(1)}, bf16[96,128]{1,0:T(8,128)(2,1)S(1)}, u32[]{:S(2)}, u32[]{:S(2)}) collective-permute-start(bf16[96,128]{1,0:T(8,128)(2,1)S(1)} %reshape.126), channel_id=1, source_target_pairs={{0,32},{16,48},{32,0},{48,16},{1,33},{17,49},{33,1},{49,17},{2,34}... | collective-permute-start | bytes 73736 | tf_op jit(solution)/shard_map/ppermute | solution.py:26
  34.0 6.0 %collective-permute-start.2 = (bf16[3,64,128]{2,1,0:T(8,128)(2,1)S(1)}, bf16[3,64,128]{2,1,0:T(8,128)(2,1)S(1)}, u32[]{:S(2)}, u32[]{:S(2)}) collective-permute-start(bf16[3,64,128]{2,1,0:T(8,128)(2,1)S(1)} %reshape.124), channel_id=1, source_target_pairs={{0,32},{16,48},{32,0},{48,16},{1,33},{17,49},{33,1},{49,17},{2,34}... | collective-permute-start | bytes 147464 | tf_op jit(solution)/shard_map/ppermute | solution.py:26
  57.7 12.9 %all-gather.5.cloned.1.call-done = bf16[4,1536,128]{2,1,0:T(8,128)(2,1)} async-done(((bf16[4,96,128]{2,1,0:T(8,128)(2,1)}), bf16[4,1536,128]{2,1,0:T(8,128)(2,1)}) %all-gather.5.cloned.1.call-update) | async-done | bytes 1572880 | tf_op jit(solution)/shard_map/all_gather | solution.py:45
  70.6 5.1 reshape_reshape.3
  75.7 4.3 copy.17
  80.0 34.8 %all-gather.3.cloned.1.call-done = bf16[4,48,64,128]{3,2,1,0:T(8,128)(2,1)} async-done(((bf16[4,3,64,128]{3,2,1,0:T(8,128)(2,1)}), bf16[4,48,64,128]{3,2,1,0:T(8,128)(2,1)}) %all-gather.3.cloned.1.call-update) | async-done | bytes 3145744 | tf_op jit(solution)/shard_map/all_gather | solution.py:37
  114.8 388.7 %while.16 = (s32[]{:T(128)}, bf16[16,6144]{1,0:T(8,128)(2,1)S(1)}, bf16[8,16,6144]{2,1,0:T(8,128)(2,1)}, s32[]{:T(128)}, pred[]{:T(512)}, /*index=5*/bf16[8,16,6...) while((s32[]{:T(128)}, bf16[16,6144]{1,0:T(8,128)(2,1)S(1)}, ...), condition=%wide.region_7.8_spmd, body=%wide.region_3.7_spmd.sunk | while | flops 78450392 | bytes 21276344 | solution.py:113
  117.8 5.9 %collective-permute-done = bf16[16,6144]{1,0:T(8,128)(2,1)S(1)} collective-permute-done((bf16[16,6144]{1,0:T(8,128)(2,1)S(1)}, bf16[16,6144]{1,0:T(8,128)(2,1)S(1)}, u32[]{:S(2)}, u32[]{:S(2)}) %collective-permute-start) | collective-permute-done | bytes 196640 | tf_op jit(solution)/shard_map/while/body/eval_jaxpr/ppermute | solution.py:18
  126.8 5.1 collective-permute-done
  134.9 4.6 collective-permute-done
  142.5 4.6 collective-permute-done
  150.1 4.7 collective-permute-done
  157.8 6.7 %collective-permute-done = bf16[16,6144]{1,0:T(8,128)(2,1)S(1)} collective-permute-done((bf16[16,6144]{1,0:T(8,128)(2,1)S(1)}, bf16[16,6144]{1,0:T(8,128)(2,1)S(1)}, u32[]{:S(2)}, u32[]{:S(2)}) %collective-permute-start) | collective-permute-done | bytes 196640 | tf_op jit(solution)/shard_map/while/body/eval_jaxpr/ppermute | solution.py:18
  167.5 119.1 %collective-permute-done = bf16[16,6144]{1,0:T(8,128)(2,1)S(1)} collective-permute-done((bf16[16,6144]{1,0:T(8,128)(2,1)S(1)}, bf16[16,6144]{1,0:T(8,128)(2,1)S(1)}, u32[]{:S(2)}, u32[]{:S(2)}) %collective-permute-start) | collective-permute-done | bytes 196640 | tf_op jit(solution)/shard_map/while/body/eval_jaxpr/ppermute | solution.py:18
  286.6 17.7 %conditional.2 = (bf16[16,6144]{1,0:T(8,128)(2,1)S(1)}) conditional(s32[]{:T(128)} %convert_element_type.52, () %tuple.47, (pred[]{:T(512)}, s32[]{:T(128)}, bf16[8,16,6144]{2,1,0:T(8,128)(2,1)}, bf16[16,6144]{1,0:T(8,128)(2,1)S(1)}, f32[6144]{0:T(1024)}, /*index=5*/s32[384]{0:T(512)S(1)}, bf16[192,64,128]{2,1,0:T(8,128)(2,1)}, s32[192]{0:T(256)S(1)}, ...), branch_computations={%region_4.4_spmd, %region_5.6_spmd} | conditional | flops 78352080 | bytes 19506548 | solution.py:99
  307.3 6.7 %collective-permute-done = bf16[16,6144]{1,0:T(8,128)(2,1)S(1)} collective-permute-done((bf16[16,6144]{1,0:T(8,128)(2,1)S(1)}, bf16[16,6144]{1,0:T(8,128)(2,1)S(1)}, u32[]{:S(2)}, u32[]{:S(2)}) %collective-permute-start) | collective-permute-done | bytes 196640 | tf_op jit(solution)/shard_map/while/body/eval_jaxpr/ppermute | solution.py:18
  314.0 17.7 %conditional.2 = (bf16[16,6144]{1,0:T(8,128)(2,1)S(1)}) conditional(s32[]{:T(128)} %convert_element_type.52, () %tuple.47, (pred[]{:T(512)}, s32[]{:T(128)}, bf16[8,16,6144]{2,1,0:T(8,128)(2,1)}, bf16[16,6144]{1,0:T(8,128)(2,1)S(1)}, f32[6144]{0:T(1024)}, /*index=5*/s32[384]{0:T(512)S(1)}, bf16[192,64,128]{2,1,0:T(8,128)(2,1)}, s32[192]{0:T(256)S(1)}, ...), branch_computations={%region_4.4_spmd, %region_5.6_spmd} | conditional | flops 78352080 | bytes 19506548 | solution.py:99
  334.7 6.7 %collective-permute-done = bf16[16,6144]{1,0:T(8,128)(2,1)S(1)} collective-permute-done((bf16[16,6144]{1,0:T(8,128)(2,1)S(1)}, bf16[16,6144]{1,0:T(8,128)(2,1)S(1)}, u32[]{:S(2)}, u32[]{:S(2)}) %collective-permute-start) | collective-permute-done | bytes 196640 | tf_op jit(solution)/shard_map/while/body/eval_jaxpr/ppermute | solution.py:18
  341.3 17.7 %conditional.2 = (bf16[16,6144]{1,0:T(8,128)(2,1)S(1)}) conditional(s32[]{:T(128)} %convert_element_type.52, () %tuple.47, (pred[]{:T(512)}, s32[]{:T(128)}, bf16[8,16,6144]{2,1,0:T(8,128)(2,1)}, bf16[16,6144]{1,0:T(8,128)(2,1)S(1)}, f32[6144]{0:T(1024)}, /*index=5*/s32[384]{0:T(512)S(1)}, bf16[192,64,128]{2,1,0:T(8,128)(2,1)}, s32[192]{0:T(256)S(1)}, ...), branch_computations={%region_4.4_spmd, %region_5.6_spmd} | conditional | flops 78352080 | bytes 19506548 | solution.py:99
  362.0 6.7 %collective-permute-done = bf16[16,6144]{1,0:T(8,128)(2,1)S(1)} collective-permute-done((bf16[16,6144]{1,0:T(8,128)(2,1)S(1)}, bf16[16,6144]{1,0:T(8,128)(2,1)S(1)}, u32[]{:S(2)}, u32[]{:S(2)}) %collective-permute-start) | collective-permute-done | bytes 196640 | tf_op jit(solution)/shard_map/while/body/eval_jaxpr/ppermute | solution.py:18
  368.7 17.7 %conditional.2 = (bf16[16,6144]{1,0:T(8,128)(2,1)S(1)}) conditional(s32[]{:T(128)} %convert_element_type.52, () %tuple.47, (pred[]{:T(512)}, s32[]{:T(128)}, bf16[8,16,6144]{2,1,0:T(8,128)(2,1)}, bf16[16,6144]{1,0:T(8,128)(2,1)S(1)}, f32[6144]{0:T(1024)}, /*index=5*/s32[384]{0:T(512)S(1)}, bf16[192,64,128]{2,1,0:T(8,128)(2,1)}, s32[192]{0:T(256)S(1)}, ...), branch_computations={%region_4.4_spmd, %region_5.6_spmd} | conditional | flops 78352080 | bytes 19506548 | solution.py:99
  389.4 6.7 %collective-permute-done = bf16[16,6144]{1,0:T(8,128)(2,1)S(1)} collective-permute-done((bf16[16,6144]{1,0:T(8,128)(2,1)S(1)}, bf16[16,6144]{1,0:T(8,128)(2,1)S(1)}, u32[]{:S(2)}, u32[]{:S(2)}) %collective-permute-start) | collective-permute-done | bytes 196640 | tf_op jit(solution)/shard_map/while/body/eval_jaxpr/ppermute | solution.py:18
  396.1 17.7 %conditional.2 = (bf16[16,6144]{1,0:T(8,128)(2,1)S(1)}) conditional(s32[]{:T(128)} %convert_element_type.52, () %tuple.47, (pred[]{:T(512)}, s32[]{:T(128)}, bf16[8,16,6144]{2,1,0:T(8,128)(2,1)}, bf16[16,6144]{1,0:T(8,128)(2,1)S(1)}, f32[6144]{0:T(1024)}, /*index=5*/s32[384]{0:T(512)S(1)}, bf16[192,64,128]{2,1,0:T(8,128)(2,1)}, s32[192]{0:T(256)S(1)}, ...), branch_computations={%region_4.4_spmd, %region_5.6_spmd} | conditional | flops 78352080 | bytes 19506548 | solution.py:99
  416.8 6.7 %collective-permute-done = bf16[16,6144]{1,0:T(8,128)(2,1)S(1)} collective-permute-done((bf16[16,6144]{1,0:T(8,128)(2,1)S(1)}, bf16[16,6144]{1,0:T(8,128)(2,1)S(1)}, u32[]{:S(2)}, u32[]{:S(2)}) %collective-permute-start) | collective-permute-done | bytes 196640 | tf_op jit(solution)/shard_map/while/body/eval_jaxpr/ppermute | solution.py:18
  423.5 17.7 %conditional.2 = (bf16[16,6144]{1,0:T(8,128)(2,1)S(1)}) conditional(s32[]{:T(128)} %convert_element_type.52, () %tuple.47, (pred[]{:T(512)}, s32[]{:T(128)}, bf16[8,16,6144]{2,1,0:T(8,128)(2,1)}, bf16[16,6144]{1,0:T(8,128)(2,1)S(1)}, f32[6144]{0:T(1024)}, /*index=5*/s32[384]{0:T(512)S(1)}, bf16[192,64,128]{2,1,0:T(8,128)(2,1)}, s32[192]{0:T(256)S(1)}, ...), branch_computations={%region_4.4_spmd, %region_5.6_spmd} | conditional | flops 78352080 | bytes 19506548 | solution.py:99
  444.2 6.7 %collective-permute-done = bf16[16,6144]{1,0:T(8,128)(2,1)S(1)} collective-permute-done((bf16[16,6144]{1,0:T(8,128)(2,1)S(1)}, bf16[16,6144]{1,0:T(8,128)(2,1)S(1)}, u32[]{:S(2)}, u32[]{:S(2)}) %collective-permute-start) | collective-permute-done | bytes 196640 | tf_op jit(solution)/shard_map/while/body/eval_jaxpr/ppermute | solution.py:18
  450.8 17.7 %conditional.2 = (bf16[16,6144]{1,0:T(8,128)(2,1)S(1)}) conditional(s32[]{:T(128)} %convert_element_type.52, () %tuple.47, (pred[]{:T(512)}, s32[]{:T(128)}, bf16[8,16,6144]{2,1,0:T(8,128)(2,1)}, bf16[16,6144]{1,0:T(8,128)(2,1)S(1)}, f32[6144]{0:T(1024)}, /*index=5*/s32[384]{0:T(512)S(1)}, bf16[192,64,128]{2,1,0:T(8,128)(2,1)}, s32[192]{0:T(256)S(1)}, ...), branch_computations={%region_4.4_spmd, %region_5.6_spmd} | conditional | flops 78352080 | bytes 19506548 | solution.py:99
  471.5 6.7 %collective-permute-done = bf16[16,6144]{1,0:T(8,128)(2,1)S(1)} collective-permute-done((bf16[16,6144]{1,0:T(8,128)(2,1)S(1)}, bf16[16,6144]{1,0:T(8,128)(2,1)S(1)}, u32[]{:S(2)}, u32[]{:S(2)}) %collective-permute-start) | collective-permute-done | bytes 196640 | tf_op jit(solution)/shard_map/while/body/eval_jaxpr/ppermute | solution.py:18
  478.2 17.7 %conditional.2 = (bf16[16,6144]{1,0:T(8,128)(2,1)S(1)}) conditional(s32[]{:T(128)} %convert_element_type.52, () %tuple.47, (pred[]{:T(512)}, s32[]{:T(128)}, bf16[8,16,6144]{2,1,0:T(8,128)(2,1)}, bf16[16,6144]{1,0:T(8,128)(2,1)S(1)}, f32[6144]{0:T(1024)}, /*index=5*/s32[384]{0:T(512)S(1)}, bf16[192,64,128]{2,1,0:T(8,128)(2,1)}, s32[192]{0:T(256)S(1)}, ...), branch_computations={%region_4.4_spmd, %region_5.6_spmd} | conditional | flops 78352080 | bytes 19506548 | solution.py:99
  498.9 4.6 collective-permute-done
  503.5 4.7 scatter_fusion
  (313 shorter events, 217.6 us)
Async XLA Ops:
  6.5 24.0 %copy-start.4 = (bf16[1,6,4096]{2,1,0:T(8,128)(2,1)S(1)}, bf16[1,6,4096]{2,1,0:T(8,128)(2,1)}, u32[]{:S(2)}) copy-start(bf16[1,6,4096]{2,1,0:T(8,128)(2,1)} %param.15) | copy-start | bytes 147460
  6.5 1.6 copy-start.3
  6.5 64.1 %all-gather.5.cloned.1.call-start = ((), (), s32[]{:S(2)}) async-start(), calls=%async_computation.1 | async-start | bytes 1671168 | tf_op jit(solution)/shard_map/all_gather | solution.py:45
  8.1 40.2 %copy-start.6 = (s32[160]{0:T(256)S(1)}, s32[160]{0:T(256)}, u32[]{:S(2)}) copy-start(s32[160]{0:T(256)} %param.12) | copy-start | bytes 1924
  8.2 18.1 %collective-permute-start.4 = (bf16[96,128]{1,0:T(8,128)(2,1)S(1)}, bf16[96,128]{1,0:T(8,128)(2,1)S(1)}, u32[]{:S(2)}, u32[]{:S(2)}) collective-permute-start(bf16[96,128]{1,0:T(8,128)(2,1)S(1)} %reshape.126), channel_id=1, source_target_pairs={{0,16},{16,32},{32,48},{48,0},{1,17},{17,33},{33,49},{49,1},{2,18}... | collective-permute-start | bytes 73736 | tf_op jit(solution)/shard_map/ppermute | solution.py:26
  14.3 12.0 %collective-permute-start.5 = (bf16[96,128]{1,0:T(8,128)(2,1)S(1)}, bf16[96,128]{1,0:T(8,128)(2,1)S(1)}, u32[]{:S(2)}, u32[]{:S(2)}) collective-permute-start(bf16[96,128]{1,0:T(8,128)(2,1)S(1)} %reshape.126), channel_id=1, source_target_pairs={{0,32},{16,48},{32,0},{48,16},{1,33},{17,49},{33,1},{49,17},{2,34}... | collective-permute-start | bytes 73736 | tf_op jit(solution)/shard_map/ppermute | solution.py:26
  22.5 6.6 %collective-permute-start.6 = (bf16[96,128]{1,0:T(8,128)(2,1)S(1)}, bf16[96,128]{1,0:T(8,128)(2,1)S(1)}, u32[]{:S(2)}, u32[]{:S(2)}) collective-permute-start(bf16[96,128]{1,0:T(8,128)(2,1)S(1)} %reshape.126), channel_id=1, source_target_pairs={{0,48},{16,0},{32,16},{48,32},{1,49},{17,1},{33,17},{49,33},{2,50}... | collective-permute-start | bytes 73736 | tf_op jit(solution)/shard_map/ppermute | solution.py:26
  30.5 84.3 %all-gather.3.cloned.1.call-start = ((), (), s32[]{:S(2)}) async-start(), calls=%async_computation | async-start | bytes 3342336 | tf_op jit(solution)/shard_map/all_gather | solution.py:37
  30.9 11.3 %collective-permute-start.1 = (bf16[3,64,128]{2,1,0:T(8,128)(2,1)S(1)}, bf16[3,64,128]{2,1,0:T(8,128)(2,1)S(1)}, u32[]{:S(2)}, u32[]{:S(2)}) collective-permute-start(bf16[3,64,128]{2,1,0:T(8,128)(2,1)S(1)} %reshape.124), channel_id=1, source_target_pairs={{0,16},{16,32},{32,48},{48,0},{1,17},{17,33},{33,49},{49,1},{2,18}... | collective-permute-start | bytes 147464 | tf_op jit(solution)/shard_map/ppermute | solution.py:26
  34.0 10.3 %collective-permute-start.2 = (bf16[3,64,128]{2,1,0:T(8,128)(2,1)S(1)}, bf16[3,64,128]{2,1,0:T(8,128)(2,1)S(1)}, u32[]{:S(2)}, u32[]{:S(2)}) collective-permute-start(bf16[3,64,128]{2,1,0:T(8,128)(2,1)S(1)} %reshape.124), channel_id=1, source_target_pairs={{0,32},{16,48},{32,0},{48,16},{1,33},{17,49},{33,1},{49,17},{2,34}... | collective-permute-start | bytes 147464 | tf_op jit(solution)/shard_map/ppermute | solution.py:26
  40.0 6.9 %collective-permute-start.3 = (bf16[3,64,128]{2,1,0:T(8,128)(2,1)S(1)}, bf16[3,64,128]{2,1,0:T(8,128)(2,1)S(1)}, u32[]{:S(2)}, u32[]{:S(2)}) collective-permute-start(bf16[3,64,128]{2,1,0:T(8,128)(2,1)S(1)} %reshape.124), channel_id=1, source_target_pairs={{0,48},{16,0},{32,16},{48,32},{1,49},{17,1},{33,17},{49,33},{2,50}... | collective-permute-start | bytes 147464 | tf_op jit(solution)/shard_map/ppermute | solution.py:26
  53.7 2.8 copy-start.7
  53.7 3.1 copy-start.8
  53.7 3.3 copy-start.5
  114.9 8.9 %collective-permute-start = (bf16[16,6144]{1,0:T(8,128)(2,1)S(1)}, bf16[16,6144]{1,0:T(8,128)(2,1)S(1)}, u32[]{:S(2)}, u32[]{:S(2)}) collective-permute-start(bf16[16,6144]{1,0:T(8,128)(2,1)S(1)} %get-tuple-element.467), channel_id=1, source_target_pairs={{0,64},{64,128},{128,192},{192,256},{256,320},{320,384},{384,448},... | collective-permute-start | bytes 589832 | tf_op jit(solution)/shard_map/while/body/eval_jaxpr/ppermute | solution.py:18
  123.8 8.1 %collective-permute-start = (bf16[16,6144]{1,0:T(8,128)(2,1)S(1)}, bf16[16,6144]{1,0:T(8,128)(2,1)S(1)}, u32[]{:S(2)}, u32[]{:S(2)}) collective-permute-start(bf16[16,6144]{1,0:T(8,128)(2,1)S(1)} %get-tuple-element.467), channel_id=1, source_target_pairs={{0,64},{64,128},{128,192},{192,256},{256,320},{320,384},{384,448},... | collective-permute-start | bytes 589832 | tf_op jit(solution)/shard_map/while/body/eval_jaxpr/ppermute | solution.py:18
  131.9 7.6 %collective-permute-start = (bf16[16,6144]{1,0:T(8,128)(2,1)S(1)}, bf16[16,6144]{1,0:T(8,128)(2,1)S(1)}, u32[]{:S(2)}, u32[]{:S(2)}) collective-permute-start(bf16[16,6144]{1,0:T(8,128)(2,1)S(1)} %get-tuple-element.467), channel_id=1, source_target_pairs={{0,64},{64,128},{128,192},{192,256},{256,320},{320,384},{384,448},... | collective-permute-start | bytes 589832 | tf_op jit(solution)/shard_map/while/body/eval_jaxpr/ppermute | solution.py:18
  139.5 7.6 %collective-permute-start = (bf16[16,6144]{1,0:T(8,128)(2,1)S(1)}, bf16[16,6144]{1,0:T(8,128)(2,1)S(1)}, u32[]{:S(2)}, u32[]{:S(2)}) collective-permute-start(bf16[16,6144]{1,0:T(8,128)(2,1)S(1)} %get-tuple-element.467), channel_id=1, source_target_pairs={{0,64},{64,128},{128,192},{192,256},{256,320},{320,384},{384,448},... | collective-permute-start | bytes 589832 | tf_op jit(solution)/shard_map/while/body/eval_jaxpr/ppermute | solution.py:18
  147.1 7.7 %collective-permute-start = (bf16[16,6144]{1,0:T(8,128)(2,1)S(1)}, bf16[16,6144]{1,0:T(8,128)(2,1)S(1)}, u32[]{:S(2)}, u32[]{:S(2)}) collective-permute-start(bf16[16,6144]{1,0:T(8,128)(2,1)S(1)} %get-tuple-element.467), channel_id=1, source_target_pairs={{0,64},{64,128},{128,192},{192,256},{256,320},{320,384},{384,448},... | collective-permute-start | bytes 589832 | tf_op jit(solution)/shard_map/while/body/eval_jaxpr/ppermute | solution.py:18
  154.8 9.7 %collective-permute-start = (bf16[16,6144]{1,0:T(8,128)(2,1)S(1)}, bf16[16,6144]{1,0:T(8,128)(2,1)S(1)}, u32[]{:S(2)}, u32[]{:S(2)}) collective-permute-start(bf16[16,6144]{1,0:T(8,128)(2,1)S(1)} %get-tuple-element.467), channel_id=1, source_target_pairs={{0,64},{64,128},{128,192},{192,256},{256,320},{320,384},{384,448},... | collective-permute-start | bytes 589832 | tf_op jit(solution)/shard_map/while/body/eval_jaxpr/ppermute | solution.py:18
  164.5 122.1 %collective-permute-start = (bf16[16,6144]{1,0:T(8,128)(2,1)S(1)}, bf16[16,6144]{1,0:T(8,128)(2,1)S(1)}, u32[]{:S(2)}, u32[]{:S(2)}) collective-permute-start(bf16[16,6144]{1,0:T(8,128)(2,1)S(1)} %get-tuple-element.467), channel_id=1, source_target_pairs={{0,64},{64,128},{128,192},{192,256},{256,320},{320,384},{384,448},... | collective-permute-start | bytes 589832 | tf_op jit(solution)/shard_map/while/body/eval_jaxpr/ppermute | solution.py:18
  303.3 0.9 copy-start.2
  304.3 9.7 %collective-permute-start = (bf16[16,6144]{1,0:T(8,128)(2,1)S(1)}, bf16[16,6144]{1,0:T(8,128)(2,1)S(1)}, u32[]{:S(2)}, u32[]{:S(2)}) collective-permute-start(bf16[16,6144]{1,0:T(8,128)(2,1)S(1)} %get-tuple-element.467), channel_id=1, source_target_pairs={{0,64},{64,128},{128,192},{192,256},{256,320},{320,384},{384,448},... | collective-permute-start | bytes 589832 | tf_op jit(solution)/shard_map/while/body/eval_jaxpr/ppermute | solution.py:18
  330.7 0.9 copy-start.2
  331.7 9.7 %collective-permute-start = (bf16[16,6144]{1,0:T(8,128)(2,1)S(1)}, bf16[16,6144]{1,0:T(8,128)(2,1)S(1)}, u32[]{:S(2)}, u32[]{:S(2)}) collective-permute-start(bf16[16,6144]{1,0:T(8,128)(2,1)S(1)} %get-tuple-element.467), channel_id=1, source_target_pairs={{0,64},{64,128},{128,192},{192,256},{256,320},{320,384},{384,448},... | collective-permute-start | bytes 589832 | tf_op jit(solution)/shard_map/while/body/eval_jaxpr/ppermute | solution.py:18
  359.0 9.7 %collective-permute-start = (bf16[16,6144]{1,0:T(8,128)(2,1)S(1)}, bf16[16,6144]{1,0:T(8,128)(2,1)S(1)}, u32[]{:S(2)}, u32[]{:S(2)}) collective-permute-start(bf16[16,6144]{1,0:T(8,128)(2,1)S(1)} %get-tuple-element.467), channel_id=1, source_target_pairs={{0,64},{64,128},{128,192},{192,256},{256,320},{320,384},{384,448},... | collective-permute-start | bytes 589832 | tf_op jit(solution)/shard_map/while/body/eval_jaxpr/ppermute | solution.py:18
  386.4 9.7 %collective-permute-start = (bf16[16,6144]{1,0:T(8,128)(2,1)S(1)}, bf16[16,6144]{1,0:T(8,128)(2,1)S(1)}, u32[]{:S(2)}, u32[]{:S(2)}) collective-permute-start(bf16[16,6144]{1,0:T(8,128)(2,1)S(1)} %get-tuple-element.467), channel_id=1, source_target_pairs={{0,64},{64,128},{128,192},{192,256},{256,320},{320,384},{384,448},... | collective-permute-start | bytes 589832 | tf_op jit(solution)/shard_map/while/body/eval_jaxpr/ppermute | solution.py:18
  413.8 9.7 %collective-permute-start = (bf16[16,6144]{1,0:T(8,128)(2,1)S(1)}, bf16[16,6144]{1,0:T(8,128)(2,1)S(1)}, u32[]{:S(2)}, u32[]{:S(2)}) collective-permute-start(bf16[16,6144]{1,0:T(8,128)(2,1)S(1)} %get-tuple-element.467), channel_id=1, source_target_pairs={{0,64},{64,128},{128,192},{192,256},{256,320},{320,384},{384,448},... | collective-permute-start | bytes 589832 | tf_op jit(solution)/shard_map/while/body/eval_jaxpr/ppermute | solution.py:18
  441.2 9.7 %collective-permute-start = (bf16[16,6144]{1,0:T(8,128)(2,1)S(1)}, bf16[16,6144]{1,0:T(8,128)(2,1)S(1)}, u32[]{:S(2)}, u32[]{:S(2)}) collective-permute-start(bf16[16,6144]{1,0:T(8,128)(2,1)S(1)} %get-tuple-element.467), channel_id=1, source_target_pairs={{0,64},{64,128},{128,192},{192,256},{256,320},{320,384},{384,448},... | collective-permute-start | bytes 589832 | tf_op jit(solution)/shard_map/while/body/eval_jaxpr/ppermute | solution.py:18
  468.5 9.7 %collective-permute-start = (bf16[16,6144]{1,0:T(8,128)(2,1)S(1)}, bf16[16,6144]{1,0:T(8,128)(2,1)S(1)}, u32[]{:S(2)}, u32[]{:S(2)}) collective-permute-start(bf16[16,6144]{1,0:T(8,128)(2,1)S(1)} %get-tuple-element.467), channel_id=1, source_target_pairs={{0,64},{64,128},{128,192},{192,256},{256,320},{320,384},{384,448},... | collective-permute-start | bytes 589832 | tf_op jit(solution)/shard_map/while/body/eval_jaxpr/ppermute | solution.py:18
  495.9 7.6 %collective-permute-start = (bf16[16,6144]{1,0:T(8,128)(2,1)S(1)}, bf16[16,6144]{1,0:T(8,128)(2,1)S(1)}, u32[]{:S(2)}, u32[]{:S(2)}) collective-permute-start(bf16[16,6144]{1,0:T(8,128)(2,1)S(1)} %get-tuple-element.467), channel_id=1, source_target_pairs={{0,64},{64,128},{128,192},{192,256},{256,320},{320,384},{384,448},... | collective-permute-start | bytes 589832 | tf_op jit(solution)/shard_map/while/body/eval_jaxpr/ppermute | solution.py:18
  508.2 1.3 copy-start
  (14 other events, 11.4 us)
Sparse Core Ops, SparseCore 0:
  30.6 39.9 all-gather.4
  72.7 42.0 all-gather.2
where the time goes:
time: 519 us; the launch traced here: 516 us
  waiting for transfers between devices  257 us (50%)
  local copies, waits for them, and re-layouts  116 us (22%)
  matrix products  49.8 us (10%)
  starting transfers between devices  48.6 us (9%)
  other arithmetic  29.9 us (6%)
  between operations  13.7 us (3%)
    ppermute x15, waiting for transfers between devices, from_behind(): lax.ppermute(value, axis, [(source, source + steps) for source in range(i...  202 us
    gather x16, local copies, waits for them, and re-layouts, layer(): picked = normed.reshape(count, blocks_in, BLK)[:, up_index, :]  35 us
    all_gather x1, waiting for transfers between devices, gather_up(): full = lax.all_gather(full, ('y', 'c'), axis=1, tiled=True)  34.8 us
    dot_general x8, matrix products, layer(): jnp.einsum('ncr,cjr->ncj', picked, weights_up, preferred_element_type=jnp...  31.2 us
    ppermute x6, starting transfers between devices, exchange_zh(): lax.ppermute(part, 'zh', [(i, (i + shift) % count) for i in range(count)])  29.2 us
    ppermute x15, starting transfers between devices, from_behind(): lax.ppermute(value, axis, [(source, source + steps) for source in range(i...  19.4 us
    dot_general x8, matrix products, layer(): jnp.einsum('ncr,crj->ncj', second, weights_down, preferred_element_type=j...  18.6 us
    dynamic_slice x15, local copies, waits for them, and re-layouts, advance(): current = lax.dynamic_index_in_dim(record, slot, 0, keepdims=False)  14.2 us
  transfers between devices with their start and end apart: 23, of which 20 were waited for; matrix products, arithmetic and copies ran while one was open for 9% of the time, Pallas kernels for 0%

commit v1 on v0

--- a/solution.py
+++ b/solution.py
@@ -42,7 +42,9 @@
     n = shard.shape[1]
     part = shard.reshape(n * 32, 128)
     full = exchange_zh(part)
-    full = lax.all_gather(full, ("y", "c"), axis=1, tiled=True)
+    full = jnp.concatenate(
+        lax.all_to_all(jnp.stack([full] * lax.axis_size(("y", "c"))), ("y", "c"), 0, 0), axis=1
+    )
     return full.reshape(-1, 4096)
 
 

time: 519 us -> 515 us (level)
  waiting for transfers between devices: 257 us -> 242 us
  starting transfers between devices: 48.6 us -> 56.4 us
    all_gather x1, waiting for transfers between devices: 34.8 us -> 0.01 us  [gather_up(): full = lax.all_gather(full, ('y', 'c'), axis=1, tiled=True)]
    all_to_all x0 -> x1, waiting for transfers between devices: none -> 34 us  [gather_rows(): lax.all_to_all(jnp.stack([full] * lax.axis_size(('y', 'c'))), ('y', 'c'),...]
    all_gather x1 -> x0, waiting for transfers between devices: 12.9 us -> none  [gather_rows(): full = lax.all_gather(full, ('y', 'c'), axis=1, tiled=True)]
    all_to_all x0 -> x1, starting transfers between devices: none -> 7.38 us  [gather_rows(): lax.all_to_all(jnp.stack([full] * lax.axis_size(('y', 'c'))), ('y', 'c'),...]
  transfers between devices with their start and end apart: 23 -> 23, of which waited for: 20 -> 19; matrix products, arithmetic and copies ran while one was open for 9% -> 10% of each run, Pallas kernels for 0% -> 0%
where the time goes in v1:
time: 515 us; the launch traced here: 513 us
  waiting for transfers between devices  242 us (47%)
  local copies, waits for them, and re-layouts  120 us (23%)
  starting transfers between devices  56.4 us (11%)
  matrix products  49.8 us (10%)
  other arithmetic  29.2 us (6%)
  between operations  13.7 us (3%)
    ppermute x15, waiting for transfers between devices, from_behind(): lax.ppermute(value, axis, [(source, source + steps) for source in range(i...  201 us
    gather x16, local copies, waits for them, and re-layouts, layer(): picked = normed.reshape(count, blocks_in, BLK)[:, up_index, :]  35 us
    all_to_all x1, waiting for transfers between devices, gather_rows(): lax.all_to_all(jnp.stack([full] * lax.axis_size(('y', 'c'))), ('y', 'c'),...  34 us
    dot_general x8, matrix products, layer(): jnp.einsum('ncr,cjr->ncj', picked, weights_up, preferred_element_type=jnp...  31.2 us
    ppermute x6, starting transfers between devices, exchange_zh(): lax.ppermute(part, 'zh', [(i, (i + shift) % count) for i in range(count)])  29.6 us
    ppermute x15, starting transfers between devices, from_behind(): lax.ppermute(value, axis, [(source, source + steps) for source in range(i...  19.4 us
    dot_general x8, matrix products, layer(): jnp.einsum('ncr,crj->ncj', second, weights_down, preferred_element_type=j...  18.6 us
    dynamic_slice x15, local copies, waits for them, and re-layouts, advance(): current = lax.dynamic_index_in_dim(record, slot, 0, keepdims=False)  14.2 us
  transfers between devices with their start and end apart: 23, of which 19 were waited for; matrix products, arithmetic and copies ran while one was open for 10% of the time, Pallas kernels for 0%

profile of v1, /device:TPU:70, one launch (start us, length us, event | category | flops | bytes accessed | tf_op | source)
XLA Modules:
  0.0 512.5 jit_solution(11915193510586564001)
XLA Ops:
  8.5 6.1 %collective-permute-start.1 = (bf16[3,64,128]{2,1,0:T(8,128)(2,1)S(1)}, bf16[3,64,128]{2,1,0:T(8,128)(2,1)S(1)}, u32[]{:S(2)}, u32[]{:S(2)}) collective-permute-start(bf16[3,64,128]{2,1,0:T(8,128)(2,1)S(1)} %reshape.129), channel_id=1, source_target_pairs={{0,16},{16,32},{32,48},{48,0},{1,17},{17,33},{33,49},{49,1},{2,18}... | collective-permute-start | bytes 147464 | tf_op jit(solution)/shard_map/ppermute | solution.py:26
  14.6 8.2 %collective-permute-start.2 = (bf16[3,64,128]{2,1,0:T(8,128)(2,1)S(1)}, bf16[3,64,128]{2,1,0:T(8,128)(2,1)S(1)}, u32[]{:S(2)}, u32[]{:S(2)}) collective-permute-start(bf16[3,64,128]{2,1,0:T(8,128)(2,1)S(1)} %reshape.129), channel_id=1, source_target_pairs={{0,32},{16,48},{32,0},{48,16},{1,33},{17,49},{33,1},{49,17},{2,34}... | collective-permute-start | bytes 147464 | tf_op jit(solution)/shard_map/ppermute | solution.py:26
  34.3 6.5 %collective-permute-start.5 = (bf16[96,128]{1,0:T(8,128)(2,1)S(1)}, bf16[96,128]{1,0:T(8,128)(2,1)S(1)}, u32[]{:S(2)}, u32[]{:S(2)}) collective-permute-start(bf16[96,128]{1,0:T(8,128)(2,1)S(1)} %reshape.131), channel_id=1, source_target_pairs={{0,32},{16,48},{32,0},{48,16},{1,33},{17,49},{33,1},{49,17},{2,34}... | collective-permute-start | bytes 73736 | tf_op jit(solution)/shard_map/ppermute | solution.py:26
  49.5 7.4 %all-to-all-start = ((bf16[16,4,96,128]{3,2,1,0:T(8,128)(2,1)}), bf16[16,4,96,128]{3,2,1,0:T(8,128)(2,1)}, u32[]{:S(2)}, u32[]{:S(2)}) async-start(bf16[16,4,96,128]{3,2,1,0:T(8,128)(2,1)} %stack.51), calls=%async_computation | async-start | bytes 3145728 | tf_op jit(solution)/shard_map/all_to_all | solution.py:46
  66.3 34.0 %all-to-all-done = bf16[16,4,96,128]{3,2,1,0:T(8,128)(2,1)} async-done(((bf16[16,4,96,128]{3,2,1,0:T(8,128)(2,1)}), bf16[16,4,96,128]{3,2,1,0:T(8,128)(2,1)}, u32[]{:S(2)}, u32[]{:S(2)}) %all-to-all-start) | async-done | bytes 1572896 | tf_op jit(solution)/shard_map/all_to_all | solution.py:46
  103.0 5.1 reshape_reshape_reshape.3
  108.1 4.3 copy.28
  112.3 387.4 %while.16 = (s32[]{:T(128)}, bf16[16,6144]{1,0:T(8,128)(2,1)S(1)}, bf16[8,16,6144]{2,1,0:T(8,128)(2,1)}, s32[]{:T(128)}, pred[]{:T(512)}, /*index=5*/bf16[8,16,6...) while((s32[]{:T(128)}, bf16[16,6144]{1,0:T(8,128)(2,1)S(1)}, ...), condition=%wide.region_7.8_spmd, body=%wide.region_3.7_spmd.sunk | while | flops 78450392 | bytes 21276344 | solution.py:115
  115.4 5.6 %collective-permute-done = bf16[16,6144]{1,0:T(8,128)(2,1)S(1)} collective-permute-done((bf16[16,6144]{1,0:T(8,128)(2,1)S(1)}, bf16[16,6144]{1,0:T(8,128)(2,1)S(1)}, u32[]{:S(2)}, u32[]{:S(2)}) %collective-permute-start) | collective-permute-done | bytes 196640 | tf_op jit(solution)/shard_map/while/body/eval_jaxpr/ppermute | solution.py:18
  124.0 4.8 collective-permute-done
  131.8 4.6 collective-permute-done
  139.4 4.6 collective-permute-done
  147.0 4.8 collective-permute-done
  154.7 6.7 %collective-permute-done = bf16[16,6144]{1,0:T(8,128)(2,1)S(1)} collective-permute-done((bf16[16,6144]{1,0:T(8,128)(2,1)S(1)}, bf16[16,6144]{1,0:T(8,128)(2,1)S(1)}, u32[]{:S(2)}, u32[]{:S(2)}) %collective-permute-start) | collective-permute-done | bytes 196640 | tf_op jit(solution)/shard_map/while/body/eval_jaxpr/ppermute | solution.py:18
  164.4 118.6 %collective-permute-done = bf16[16,6144]{1,0:T(8,128)(2,1)S(1)} collective-permute-done((bf16[16,6144]{1,0:T(8,128)(2,1)S(1)}, bf16[16,6144]{1,0:T(8,128)(2,1)S(1)}, u32[]{:S(2)}, u32[]{:S(2)}) %collective-permute-start) | collective-permute-done | bytes 196640 | tf_op jit(solution)/shard_map/while/body/eval_jaxpr/ppermute | solution.py:18
  283.0 17.7 %conditional.2 = (bf16[16,6144]{1,0:T(8,128)(2,1)S(1)}) conditional(s32[]{:T(128)} %convert_element_type.52, () %tuple.48, (pred[]{:T(512)}, s32[]{:T(128)}, bf16[8,16,6144]{2,1,0:T(8,128)(2,1)}, bf16[16,6144]{1,0:T(8,128)(2,1)S(1)}, f32[6144]{0:T(1024)}, /*index=5*/s32[384]{0:T(512)S(1)}, bf16[192,64,128]{2,1,0:T(8,128)(2,1)}, s32[192]{0:T(256)S(1)}, ...), branch_computations={%region_4.4_spmd, %region_5.6_spmd} | conditional | flops 78352080 | bytes 19506548 | solution.py:101
  303.7 6.7 %collective-permute-done = bf16[16,6144]{1,0:T(8,128)(2,1)S(1)} collective-permute-done((bf16[16,6144]{1,0:T(8,128)(2,1)S(1)}, bf16[16,6144]{1,0:T(8,128)(2,1)S(1)}, u32[]{:S(2)}, u32[]{:S(2)}) %collective-permute-start) | collective-permute-done | bytes 196640 | tf_op jit(solution)/shard_map/while/body/eval_jaxpr/ppermute | solution.py:18
  310.4 17.7 %conditional.2 = (bf16[16,6144]{1,0:T(8,128)(2,1)S(1)}) conditional(s32[]{:T(128)} %convert_element_type.52, () %tuple.48, (pred[]{:T(512)}, s32[]{:T(128)}, bf16[8,16,6144]{2,1,0:T(8,128)(2,1)}, bf16[16,6144]{1,0:T(8,128)(2,1)S(1)}, f32[6144]{0:T(1024)}, /*index=5*/s32[384]{0:T(512)S(1)}, bf16[192,64,128]{2,1,0:T(8,128)(2,1)}, s32[192]{0:T(256)S(1)}, ...), branch_computations={%region_4.4_spmd, %region_5.6_spmd} | conditional | flops 78352080 | bytes 19506548 | solution.py:101
  331.1 6.7 %collective-permute-done = bf16[16,6144]{1,0:T(8,128)(2,1)S(1)} collective-permute-done((bf16[16,6144]{1,0:T(8,128)(2,1)S(1)}, bf16[16,6144]{1,0:T(8,128)(2,1)S(1)}, u32[]{:S(2)}, u32[]{:S(2)}) %collective-permute-start) | collective-permute-done | bytes 196640 | tf_op jit(solution)/shard_map/while/body/eval_jaxpr/ppermute | solution.py:18
  337.7 17.7 %conditional.2 = (bf16[16,6144]{1,0:T(8,128)(2,1)S(1)}) conditional(s32[]{:T(128)} %convert_element_type.52, () %tuple.48, (pred[]{:T(512)}, s32[]{:T(128)}, bf16[8,16,6144]{2,1,0:T(8,128)(2,1)}, bf16[16,6144]{1,0:T(8,128)(2,1)S(1)}, f32[6144]{0:T(1024)}, /*index=5*/s32[384]{0:T(512)S(1)}, bf16[192,64,128]{2,1,0:T(8,128)(2,1)}, s32[192]{0:T(256)S(1)}, ...), branch_computations={%region_4.4_spmd, %region_5.6_spmd} | conditional | flops 78352080 | bytes 19506548 | solution.py:101
  358.4 6.7 %collective-permute-done = bf16[16,6144]{1,0:T(8,128)(2,1)S(1)} collective-permute-done((bf16[16,6144]{1,0:T(8,128)(2,1)S(1)}, bf16[16,6144]{1,0:T(8,128)(2,1)S(1)}, u32[]{:S(2)}, u32[]{:S(2)}) %collective-permute-start) | collective-permute-done | bytes 196640 | tf_op jit(solution)/shard_map/while/body/eval_jaxpr/ppermute | solution.py:18
  365.1 17.7 %conditional.2 = (bf16[16,6144]{1,0:T(8,128)(2,1)S(1)}) conditional(s32[]{:T(128)} %convert_element_type.52, () %tuple.48, (pred[]{:T(512)}, s32[]{:T(128)}, bf16[8,16,6144]{2,1,0:T(8,128)(2,1)}, bf16[16,6144]{1,0:T(8,128)(2,1)S(1)}, f32[6144]{0:T(1024)}, /*index=5*/s32[384]{0:T(512)S(1)}, bf16[192,64,128]{2,1,0:T(8,128)(2,1)}, s32[192]{0:T(256)S(1)}, ...), branch_computations={%region_4.4_spmd, %region_5.6_spmd} | conditional | flops 78352080 | bytes 19506548 | solution.py:101
  385.8 6.7 %collective-permute-done = bf16[16,6144]{1,0:T(8,128)(2,1)S(1)} collective-permute-done((bf16[16,6144]{1,0:T(8,128)(2,1)S(1)}, bf16[16,6144]{1,0:T(8,128)(2,1)S(1)}, u32[]{:S(2)}, u32[]{:S(2)}) %collective-permute-start) | collective-permute-done | bytes 196640 | tf_op jit(solution)/shard_map/while/body/eval_jaxpr/ppermute | solution.py:18
  392.4 17.7 %conditional.2 = (bf16[16,6144]{1,0:T(8,128)(2,1)S(1)}) conditional(s32[]{:T(128)} %convert_element_type.52, () %tuple.48, (pred[]{:T(512)}, s32[]{:T(128)}, bf16[8,16,6144]{2,1,0:T(8,128)(2,1)}, bf16[16,6144]{1,0:T(8,128)(2,1)S(1)}, f32[6144]{0:T(1024)}, /*index=5*/s32[384]{0:T(512)S(1)}, bf16[192,64,128]{2,1,0:T(8,128)(2,1)}, s32[192]{0:T(256)S(1)}, ...), branch_computations={%region_4.4_spmd, %region_5.6_spmd} | conditional | flops 78352080 | bytes 19506548 | solution.py:101
  413.1 6.7 %collective-permute-done = bf16[16,6144]{1,0:T(8,128)(2,1)S(1)} collective-permute-done((bf16[16,6144]{1,0:T(8,128)(2,1)S(1)}, bf16[16,6144]{1,0:T(8,128)(2,1)S(1)}, u32[]{:S(2)}, u32[]{:S(2)}) %collective-permute-start) | collective-permute-done | bytes 196640 | tf_op jit(solution)/shard_map/while/body/eval_jaxpr/ppermute | solution.py:18
  419.8 17.7 %conditional.2 = (bf16[16,6144]{1,0:T(8,128)(2,1)S(1)}) conditional(s32[]{:T(128)} %convert_element_type.52, () %tuple.48, (pred[]{:T(512)}, s32[]{:T(128)}, bf16[8,16,6144]{2,1,0:T(8,128)(2,1)}, bf16[16,6144]{1,0:T(8,128)(2,1)S(1)}, f32[6144]{0:T(1024)}, /*index=5*/s32[384]{0:T(512)S(1)}, bf16[192,64,128]{2,1,0:T(8,128)(2,1)}, s32[192]{0:T(256)S(1)}, ...), branch_computations={%region_4.4_spmd, %region_5.6_spmd} | conditional | flops 78352080 | bytes 19506548 | solution.py:101
  440.4 6.7 %collective-permute-done = bf16[16,6144]{1,0:T(8,128)(2,1)S(1)} collective-permute-done((bf16[16,6144]{1,0:T(8,128)(2,1)S(1)}, bf16[16,6144]{1,0:T(8,128)(2,1)S(1)}, u32[]{:S(2)}, u32[]{:S(2)}) %collective-permute-start) | collective-permute-done | bytes 196640 | tf_op jit(solution)/shard_map/while/body/eval_jaxpr/ppermute | solution.py:18
  447.1 17.7 %conditional.2 = (bf16[16,6144]{1,0:T(8,128)(2,1)S(1)}) conditional(s32[]{:T(128)} %convert_element_type.52, () %tuple.48, (pred[]{:T(512)}, s32[]{:T(128)}, bf16[8,16,6144]{2,1,0:T(8,128)(2,1)}, bf16[16,6144]{1,0:T(8,128)(2,1)S(1)}, f32[6144]{0:T(1024)}, /*index=5*/s32[384]{0:T(512)S(1)}, bf16[192,64,128]{2,1,0:T(8,128)(2,1)}, s32[192]{0:T(256)S(1)}, ...), branch_computations={%region_4.4_spmd, %region_5.6_spmd} | conditional | flops 78352080 | bytes 19506548 | solution.py:101
  467.8 6.7 %collective-permute-done = bf16[16,6144]{1,0:T(8,128)(2,1)S(1)} collective-permute-done((bf16[16,6144]{1,0:T(8,128)(2,1)S(1)}, bf16[16,6144]{1,0:T(8,128)(2,1)S(1)}, u32[]{:S(2)}, u32[]{:S(2)}) %collective-permute-start) | collective-permute-done | bytes 196640 | tf_op jit(solution)/shard_map/while/body/eval_jaxpr/ppermute | solution.py:18
  474.5 17.7 %conditional.2 = (bf16[16,6144]{1,0:T(8,128)(2,1)S(1)}) conditional(s32[]{:T(128)} %convert_element_type.52, () %tuple.48, (pred[]{:T(512)}, s32[]{:T(128)}, bf16[8,16,6144]{2,1,0:T(8,128)(2,1)}, bf16[16,6144]{1,0:T(8,128)(2,1)S(1)}, f32[6144]{0:T(1024)}, /*index=5*/s32[384]{0:T(512)S(1)}, bf16[192,64,128]{2,1,0:T(8,128)(2,1)}, s32[192]{0:T(256)S(1)}, ...), branch_computations={%region_4.4_spmd, %region_5.6_spmd} | conditional | flops 78352080 | bytes 19506548 | solution.py:101
  495.1 4.6 collective-permute-done
  499.7 4.7 scatter_fusion
  (314 shorter events, 220.7 us)
Async XLA Ops:
  6.5 1.6 copy-start.4
  6.5 105.8 %all-gather.2.cloned.1.call-start = ((), (), s32[]{:S(2)}) async-start(), calls=%async_computation.1 | async-start | bytes 3342336 | tf_op jit(solution)/shard_map/all_gather | solution.py:37
  8.1 23.4 %copy-start.3 = (bf16[1,3,4096]{2,1,0:T(4,128)(2,1)S(1)}, bf16[1,3,4096]{2,1,0:T(4,128)(2,1)}, u32[]{:S(2)}) copy-start(bf16[1,3,4096]{2,1,0:T(4,128)(2,1)} %param.17) | copy-start | bytes 73732
  8.5 18.2 %collective-permute-start.1 = (bf16[3,64,128]{2,1,0:T(8,128)(2,1)S(1)}, bf16[3,64,128]{2,1,0:T(8,128)(2,1)S(1)}, u32[]{:S(2)}, u32[]{:S(2)}) collective-permute-start(bf16[3,64,128]{2,1,0:T(8,128)(2,1)S(1)} %reshape.129), channel_id=1, source_target_pairs={{0,16},{16,32},{32,48},{48,0},{1,17},{17,33},{33,49},{49,1},{2,18}... | collective-permute-start | bytes 147464 | tf_op jit(solution)/shard_map/ppermute | solution.py:26
  14.6 12.1 %collective-permute-start.2 = (bf16[3,64,128]{2,1,0:T(8,128)(2,1)S(1)}, bf16[3,64,128]{2,1,0:T(8,128)(2,1)S(1)}, u32[]{:S(2)}, u32[]{:S(2)}) collective-permute-start(bf16[3,64,128]{2,1,0:T(8,128)(2,1)S(1)} %reshape.129), channel_id=1, source_target_pairs={{0,32},{16,48},{32,0},{48,16},{1,33},{17,49},{33,1},{49,17},{2,34}... | collective-permute-start | bytes 147464 | tf_op jit(solution)/shard_map/ppermute | solution.py:26
  22.8 7.3 %collective-permute-start.3 = (bf16[3,64,128]{2,1,0:T(8,128)(2,1)S(1)}, bf16[3,64,128]{2,1,0:T(8,128)(2,1)S(1)}, u32[]{:S(2)}, u32[]{:S(2)}) collective-permute-start(bf16[3,64,128]{2,1,0:T(8,128)(2,1)S(1)} %reshape.129), channel_id=1, source_target_pairs={{0,48},{16,0},{32,16},{48,32},{1,49},{17,1},{33,17},{49,33},{2,50}... | collective-permute-start | bytes 147464 | tf_op jit(solution)/shard_map/ppermute | solution.py:26
  31.6 11.7 %collective-permute-start.4 = (bf16[96,128]{1,0:T(8,128)(2,1)S(1)}, bf16[96,128]{1,0:T(8,128)(2,1)S(1)}, u32[]{:S(2)}, u32[]{:S(2)}) collective-permute-start(bf16[96,128]{1,0:T(8,128)(2,1)S(1)} %reshape.131), channel_id=1, source_target_pairs={{0,16},{16,32},{32,48},{48,0},{1,17},{17,33},{33,49},{49,1},{2,18}... | collective-permute-start | bytes 73736 | tf_op jit(solution)/shard_map/ppermute | solution.py:26
  34.3 9.7 %collective-permute-start.5 = (bf16[96,128]{1,0:T(8,128)(2,1)S(1)}, bf16[96,128]{1,0:T(8,128)(2,1)S(1)}, u32[]{:S(2)}, u32[]{:S(2)}) collective-permute-start(bf16[96,128]{1,0:T(8,128)(2,1)S(1)} %reshape.131), channel_id=1, source_target_pairs={{0,32},{16,48},{32,0},{48,16},{1,33},{17,49},{33,1},{49,17},{2,34}... | collective-permute-start | bytes 73736 | tf_op jit(solution)/shard_map/ppermute | solution.py:26
  40.8 6.6 %collective-permute-start.6 = (bf16[96,128]{1,0:T(8,128)(2,1)S(1)}, bf16[96,128]{1,0:T(8,128)(2,1)S(1)}, u32[]{:S(2)}, u32[]{:S(2)}) collective-permute-start(bf16[96,128]{1,0:T(8,128)(2,1)S(1)} %reshape.131), channel_id=1, source_target_pairs={{0,48},{16,0},{32,16},{48,32},{1,49},{17,1},{33,17},{49,33},{2,50}... | collective-permute-start | bytes 73736 | tf_op jit(solution)/shard_map/ppermute | solution.py:26
  49.5 7.4 %copy-start.6 = (s32[160]{0:T(256)S(1)}, s32[160]{0:T(256)}, u32[]{:S(2)}) copy-start(s32[160]{0:T(256)} %param.12) | copy-start | bytes 1924
  49.5 50.7 %all-to-all-start = ((bf16[16,4,96,128]{3,2,1,0:T(8,128)(2,1)}), bf16[16,4,96,128]{3,2,1,0:T(8,128)(2,1)}, u32[]{:S(2)}, u32[]{:S(2)}) async-start(bf16[16,4,96,128]{3,2,1,0:T(8,128)(2,1)} %stack.51), calls=%async_computation | async-start | bytes 3145728 | tf_op jit(solution)/shard_map/all_to_all | solution.py:46
  62.3 2.8 copy-start.7
  62.3 3.1 copy-start.8
  62.3 3.3 copy-start.5
  112.4 8.6 %collective-permute-start = (bf16[16,6144]{1,0:T(8,128)(2,1)S(1)}, bf16[16,6144]{1,0:T(8,128)(2,1)S(1)}, u32[]{:S(2)}, u32[]{:S(2)}) collective-permute-start(bf16[16,6144]{1,0:T(8,128)(2,1)S(1)} %get-tuple-element.478), channel_id=1, source_target_pairs={{0,64},{64,128},{128,192},{192,256},{256,320},{320,384},{384,448},... | collective-permute-start | bytes 589832 | tf_op jit(solution)/shard_map/while/body/eval_jaxpr/ppermute | solution.py:18
  121.0 7.8 %collective-permute-start = (bf16[16,6144]{1,0:T(8,128)(2,1)S(1)}, bf16[16,6144]{1,0:T(8,128)(2,1)S(1)}, u32[]{:S(2)}, u32[]{:S(2)}) collective-permute-start(bf16[16,6144]{1,0:T(8,128)(2,1)S(1)} %get-tuple-element.478), channel_id=1, source_target_pairs={{0,64},{64,128},{128,192},{192,256},{256,320},{320,384},{384,448},... | collective-permute-start | bytes 589832 | tf_op jit(solution)/shard_map/while/body/eval_jaxpr/ppermute | solution.py:18
  128.8 7.6 %collective-permute-start = (bf16[16,6144]{1,0:T(8,128)(2,1)S(1)}, bf16[16,6144]{1,0:T(8,128)(2,1)S(1)}, u32[]{:S(2)}, u32[]{:S(2)}) collective-permute-start(bf16[16,6144]{1,0:T(8,128)(2,1)S(1)} %get-tuple-element.478), channel_id=1, source_target_pairs={{0,64},{64,128},{128,192},{192,256},{256,320},{320,384},{384,448},... | collective-permute-start | bytes 589832 | tf_op jit(solution)/shard_map/while/body/eval_jaxpr/ppermute | solution.py:18
  136.4 7.6 %collective-permute-start = (bf16[16,6144]{1,0:T(8,128)(2,1)S(1)}, bf16[16,6144]{1,0:T(8,128)(2,1)S(1)}, u32[]{:S(2)}, u32[]{:S(2)}) collective-permute-start(bf16[16,6144]{1,0:T(8,128)(2,1)S(1)} %get-tuple-element.478), channel_id=1, source_target_pairs={{0,64},{64,128},{128,192},{192,256},{256,320},{320,384},{384,448},... | collective-permute-start | bytes 589832 | tf_op jit(solution)/shard_map/while/body/eval_jaxpr/ppermute | solution.py:18
  144.0 7.7 %collective-permute-start = (bf16[16,6144]{1,0:T(8,128)(2,1)S(1)}, bf16[16,6144]{1,0:T(8,128)(2,1)S(1)}, u32[]{:S(2)}, u32[]{:S(2)}) collective-permute-start(bf16[16,6144]{1,0:T(8,128)(2,1)S(1)} %get-tuple-element.478), channel_id=1, source_target_pairs={{0,64},{64,128},{128,192},{192,256},{256,320},{320,384},{384,448},... | collective-permute-start | bytes 589832 | tf_op jit(solution)/shard_map/while/body/eval_jaxpr/ppermute | solution.py:18
  151.7 9.7 %collective-permute-start = (bf16[16,6144]{1,0:T(8,128)(2,1)S(1)}, bf16[16,6144]{1,0:T(8,128)(2,1)S(1)}, u32[]{:S(2)}, u32[]{:S(2)}) collective-permute-start(bf16[16,6144]{1,0:T(8,128)(2,1)S(1)} %get-tuple-element.478), channel_id=1, source_target_pairs={{0,64},{64,128},{128,192},{192,256},{256,320},{320,384},{384,448},... | collective-permute-start | bytes 589832 | tf_op jit(solution)/shard_map/while/body/eval_jaxpr/ppermute | solution.py:18
  161.4 121.6 %collective-permute-start = (bf16[16,6144]{1,0:T(8,128)(2,1)S(1)}, bf16[16,6144]{1,0:T(8,128)(2,1)S(1)}, u32[]{:S(2)}, u32[]{:S(2)}) collective-permute-start(bf16[16,6144]{1,0:T(8,128)(2,1)S(1)} %get-tuple-element.478), channel_id=1, source_target_pairs={{0,64},{64,128},{128,192},{192,256},{256,320},{320,384},{384,448},... | collective-permute-start | bytes 589832 | tf_op jit(solution)/shard_map/while/body/eval_jaxpr/ppermute | solution.py:18
  299.7 0.9 copy-start.2
  300.7 9.7 %collective-permute-start = (bf16[16,6144]{1,0:T(8,128)(2,1)S(1)}, bf16[16,6144]{1,0:T(8,128)(2,1)S(1)}, u32[]{:S(2)}, u32[]{:S(2)}) collective-permute-start(bf16[16,6144]{1,0:T(8,128)(2,1)S(1)} %get-tuple-element.478), channel_id=1, source_target_pairs={{0,64},{64,128},{128,192},{192,256},{256,320},{320,384},{384,448},... | collective-permute-start | bytes 589832 | tf_op jit(solution)/shard_map/while/body/eval_jaxpr/ppermute | solution.py:18
  327.1 0.9 copy-start.2
  328.1 9.7 %collective-permute-start = (bf16[16,6144]{1,0:T(8,128)(2,1)S(1)}, bf16[16,6144]{1,0:T(8,128)(2,1)S(1)}, u32[]{:S(2)}, u32[]{:S(2)}) collective-permute-start(bf16[16,6144]{1,0:T(8,128)(2,1)S(1)} %get-tuple-element.478), channel_id=1, source_target_pairs={{0,64},{64,128},{128,192},{192,256},{256,320},{320,384},{384,448},... | collective-permute-start | bytes 589832 | tf_op jit(solution)/shard_map/while/body/eval_jaxpr/ppermute | solution.py:18
  355.4 9.7 %collective-permute-start = (bf16[16,6144]{1,0:T(8,128)(2,1)S(1)}, bf16[16,6144]{1,0:T(8,128)(2,1)S(1)}, u32[]{:S(2)}, u32[]{:S(2)}) collective-permute-start(bf16[16,6144]{1,0:T(8,128)(2,1)S(1)} %get-tuple-element.478), channel_id=1, source_target_pairs={{0,64},{64,128},{128,192},{192,256},{256,320},{320,384},{384,448},... | collective-permute-start | bytes 589832 | tf_op jit(solution)/shard_map/while/body/eval_jaxpr/ppermute | solution.py:18
  382.8 9.7 %collective-permute-start = (bf16[16,6144]{1,0:T(8,128)(2,1)S(1)}, bf16[16,6144]{1,0:T(8,128)(2,1)S(1)}, u32[]{:S(2)}, u32[]{:S(2)}) collective-permute-start(bf16[16,6144]{1,0:T(8,128)(2,1)S(1)} %get-tuple-element.478), channel_id=1, source_target_pairs={{0,64},{64,128},{128,192},{192,256},{256,320},{320,384},{384,448},... | collective-permute-start | bytes 589832 | tf_op jit(solution)/shard_map/while/body/eval_jaxpr/ppermute | solution.py:18
  410.1 9.7 %collective-permute-start = (bf16[16,6144]{1,0:T(8,128)(2,1)S(1)}, bf16[16,6144]{1,0:T(8,128)(2,1)S(1)}, u32[]{:S(2)}, u32[]{:S(2)}) collective-permute-start(bf16[16,6144]{1,0:T(8,128)(2,1)S(1)} %get-tuple-element.478), channel_id=1, source_target_pairs={{0,64},{64,128},{128,192},{192,256},{256,320},{320,384},{384,448},... | collective-permute-start | bytes 589832 | tf_op jit(solution)/shard_map/while/body/eval_jaxpr/ppermute | solution.py:18
  437.4 9.7 %collective-permute-start = (bf16[16,6144]{1,0:T(8,128)(2,1)S(1)}, bf16[16,6144]{1,0:T(8,128)(2,1)S(1)}, u32[]{:S(2)}, u32[]{:S(2)}) collective-permute-start(bf16[16,6144]{1,0:T(8,128)(2,1)S(1)} %get-tuple-element.478), channel_id=1, source_target_pairs={{0,64},{64,128},{128,192},{192,256},{256,320},{320,384},{384,448},... | collective-permute-start | bytes 589832 | tf_op jit(solution)/shard_map/while/body/eval_jaxpr/ppermute | solution.py:18
  464.8 9.7 %collective-permute-start = (bf16[16,6144]{1,0:T(8,128)(2,1)S(1)}, bf16[16,6144]{1,0:T(8,128)(2,1)S(1)}, u32[]{:S(2)}, u32[]{:S(2)}) collective-permute-start(bf16[16,6144]{1,0:T(8,128)(2,1)S(1)} %get-tuple-element.478), channel_id=1, source_target_pairs={{0,64},{64,128},{128,192},{192,256},{256,320},{320,384},{384,448},... | collective-permute-start | bytes 589832 | tf_op jit(solution)/shard_map/while/body/eval_jaxpr/ppermute | solution.py:18
  492.1 7.6 %collective-permute-start = (bf16[16,6144]{1,0:T(8,128)(2,1)S(1)}, bf16[16,6144]{1,0:T(8,128)(2,1)S(1)}, u32[]{:S(2)}, u32[]{:S(2)}) collective-permute-start(bf16[16,6144]{1,0:T(8,128)(2,1)S(1)} %get-tuple-element.478), channel_id=1, source_target_pairs={{0,64},{64,128},{128,192},{192,256},{256,320},{320,384},{384,448},... | collective-permute-start | bytes 589832 | tf_op jit(solution)/shard_map/while/body/eval_jaxpr/ppermute | solution.py:18
  504.4 1.3 copy-start
  (14 other events, 11.2 us)
Sparse Core Ops, SparseCore 0:
  31.7 56.9 all-gather.1
